TPU v7x, 32 devices: a whole 2x2x4 slice. The times are simulated.
32 devices in a mesh: seq: 8 (over y, x, core), head: 4 (over z).
Axes of the slice: x: 2, y: 2, z: 4, core: 2. Of those that a mesh axis runs over, the one named last changes fastest.
Arguments:
- tokens: bfloat16 [4096, 5376], P('seq', 'head'), may hold values from -32 to 32
- query_weight: bfloat16 [5376, 4096], P(None, 'head'), may hold values from -1 to 1
- key_weight: bfloat16 [5376, 2048], P(None, 'head'), may hold values from -1 to 1
- value_weight: bfloat16 [5376, 2048], P(None, 'head'), may hold values from -0.078125 to 0.078125
- output_grad: bfloat16 [4096, 4096], P('seq', 'head'), may hold values from -48 to 48
- segments: int32 [4096], replicated, may hold values from 0 to 3, never falling along the last dimension, each value on 1 to 2048 neighbouring positions
Outputs:
- token_grad: bfloat16 [4096, 5376], P('seq', 'head')
- query_weight_grad: bfloat16 [5376, 4096], P('seq', 'head')
- key_weight_grad: bfloat16 [5376, 2048], P('seq', 'head')
- value_weight_grad: bfloat16 [5376, 2048], P('seq', 'head')
Inputs may be any that keep to these rules, and one draw needn't show every extreme that they name: `segments`: segment numbers never fall along the tokens; a segment has at most 2048 tokens.
All inputs are finite; a program needn't handle non-finite values.
Results may differ from a plain program's by a relative error of at most 0.015.
The roundings to bfloat16 on the way count: a program that leaves them out, or rounds other values in their place, can miss the bound.
Values may be sent and summed in bfloat16 or wider, within the bound.
No kernel may reach another device: no remote copies, remote signals or barrier semaphores. Data moves between devices by JAX's collectives and lax.ppermute only.
A program may use at most 192 MiB of HBM per device.

v0:
```python
import jax
import jax.numpy as jnp
from jax import lax
from jax.sharding import Mesh, PartitionSpec as P

D = 5376
HEADS = 32
KV_HEADS = 16
HEAD_DIM = 128
WINDOW = 1024
HOPS = 2
SEQ = ("seq_hi", "core")
neg_large = -1e30


def passed_along(x, axis, by):
    count = lax.axis_size(axis)
    pairs = [(i, i + by) for i in range(count) if 0 <= i + by < count]
    return lax.ppermute(x, axis, pairs)


def contract_last(left, right):
    return lax.dot_general(
        left, right, (((1,), (1,)), ((), ())), preferred_element_type=jnp.float32
    )


def contract_first(left, right):
    return lax.dot_general(
        left, right, (((0,), (0,)), ((), ())), preferred_element_type=jnp.float32
    )


def attend(queries, key_value, grads, query_first, key_first, seg_query, seg_key):
    tok_rows = queries.shape[0]
    key_rows = key_value.shape[1]
    groups = HEADS // KV_HEADS
    kv_local = key_value.shape[2] // HEAD_DIM
    score_scale = (D / HEADS) ** (-0.5)
    query_four = queries.reshape(tok_rows, kv_local, groups, HEAD_DIM)
    grad_four = grads.reshape(tok_rows, kv_local, groups, HEAD_DIM)
    key_three = key_value[0].reshape(key_rows, kv_local, HEAD_DIM)
    value_three = key_value[1].reshape(key_rows, kv_local, HEAD_DIM)
    query_pos = query_first + jnp.arange(tok_rows, dtype=jnp.int32)
    key_pos = key_first + jnp.arange(key_rows, dtype=jnp.int32)
    spacing = query_pos[:, None] - key_pos[None, :]
    allowed = (
        (key_pos >= 0)[None, :]
        & (spacing >= 0)
        & (spacing < WINDOW)
        & (seg_query[:, None] == seg_key[None, :])
    )
    scores = (
        jnp.einsum("akgd,ckd->kgac", query_four, key_three, preferred_element_type=jnp.float32)
        * score_scale
    )
    masked = jnp.where(allowed, scores, neg_large)
    row_max = jnp.max(masked, axis=-1, keepdims=True)
    expo = jnp.where(allowed, jnp.exp(masked - row_max), 0.0)
    probs = expo / jnp.sum(expo, axis=-1, keepdims=True)
    dprobs = jnp.einsum(
        "akgd,ckd->kgac", grad_four, value_three, preferred_element_type=jnp.float32
    )
    center = jnp.sum(probs * dprobs, axis=-1, keepdims=True)
    dscores = (probs * (dprobs - center)).astype(jnp.bfloat16)
    probs_low = probs.astype(jnp.bfloat16)
    query_grad = (
        (
            jnp.einsum("kgac,ckd->akgd", dscores, key_three, preferred_element_type=jnp.float32)
            * score_scale
        )
        .reshape(tok_rows, -1)
        .astype(jnp.bfloat16)
    )
    key_grad = (
        jnp.einsum("kgac,akgd->ckd", dscores, query_four, preferred_element_type=jnp.float32)
        * score_scale
    ).reshape(key_rows, -1)
    value_grad = jnp.einsum(
        "kgac,akgd->ckd", probs_low, grad_four, preferred_element_type=jnp.float32
    ).reshape(key_rows, -1)
    return (query_grad, jnp.stack([key_grad, value_grad]))


def per_device(tokens, query_weight, key_weight, value_weight, output_grad, segments):
    tok_rows = tokens.shape[0]
    hop_count = HOPS
    margin = hop_count * tok_rows
    gathered = lax.all_gather(tokens, "head", axis=1, tiled=True)
    queries = jnp.dot(gathered, query_weight, preferred_element_type=jnp.float32).astype(
        jnp.bfloat16
    )
    keys_own = jnp.dot(gathered, key_weight, preferred_element_type=jnp.float32).astype(
        jnp.bfloat16
    )
    values_own = jnp.dot(gathered, value_weight, preferred_element_type=jnp.float32).astype(
        jnp.bfloat16
    )
    key_value = jnp.stack([keys_own, values_own])
    blocks = [key_value] * (hop_count + 1)
    for distance in range(1, hop_count + 1):
        blocks[hop_count - distance] = passed_along(key_value, SEQ, distance)
    keys_all = jnp.concatenate(blocks, axis=1)
    position = lax.axis_index(SEQ)
    query_first = position * tok_rows
    seg_query = lax.dynamic_slice_in_dim(segments, query_first, tok_rows, 0)
    seg_padded = jnp.concatenate([jnp.full((margin,), -1, jnp.int32), segments], axis=0)
    seg_key = lax.dynamic_slice_in_dim(seg_padded, query_first, (hop_count + 1) * tok_rows, 0)
    query_grad, kv_grad = attend(
        queries, keys_all, output_grad, query_first, query_first - margin, seg_query, seg_key
    )
    pieces = [
        kv_grad[:, block * tok_rows : (block + 1) * tok_rows] for block in range(hop_count + 1)
    ]
    carried = pieces[hop_count]
    for distance in range(1, hop_count + 1):
        back = passed_along(pieces[hop_count - distance].astype(jnp.bfloat16), SEQ, -distance)
        carried = carried + back.astype(jnp.float32)
    key_grad = carried[0].astype(jnp.bfloat16)
    value_grad = carried[1].astype(jnp.bfloat16)
    n_head = lax.axis_size("head")
    me = lax.axis_index("head")
    width = tokens.shape[1]

    def term(dest):
        start = dest * width
        part = contract_last(query_grad, lax.dynamic_slice_in_dim(query_weight, start, width, 0))
        part = part + contract_last(key_grad, lax.dynamic_slice_in_dim(key_weight, start, width, 0))
        part = part + contract_last(
            value_grad, lax.dynamic_slice_in_dim(value_weight, start, width, 0)
        )
        return part.astype(jnp.bfloat16)

    token_sum = None
    for shift in range(n_head - 1, 0, -1):
        sent = term((me + shift) % n_head)
        pairs = [(i, (i + shift) % n_head) for i in range(n_head)]
        got = lax.ppermute(sent, "head", pairs).astype(jnp.float32)
        token_sum = got if token_sum is None else token_sum + got
    own = term(me).astype(jnp.float32)
    token_grad = (own if token_sum is None else token_sum + own).astype(jnp.bfloat16)
    proj_grads = jnp.concatenate([query_grad, key_grad, value_grad], axis=1)
    weight_part = contract_first(proj_grads, gathered).astype(jnp.bfloat16)
    n_seq = lax.axis_size(SEQ)
    block = weight_part.shape[1] // n_seq

    def weight_block(dest):
        return lax.dynamic_slice_in_dim(weight_part, dest * block, block, 1)

    weight_sum = weight_block(position).astype(jnp.float32)
    for shift in range(n_seq - 1, 0, -1):
        sent = weight_block((position + shift) % n_seq)
        pairs = [(i, (i + shift) % n_seq) for i in range(n_seq)]
        weight_sum = weight_sum + lax.ppermute(sent, SEQ, pairs).astype(jnp.float32)
    summed = (weight_sum * (tok_rows * n_seq) ** (-0.5)).astype(jnp.bfloat16).T
    q_width = query_weight.shape[1]
    k_width = key_weight.shape[1]
    query_weight_grad = summed[:, :q_width]
    key_weight_grad = summed[:, q_width : q_width + k_width]
    value_weight_grad = summed[:, q_width + k_width :]
    return (token_grad, query_weight_grad, key_weight_grad, value_weight_grad)


def solution(mesh):
    n_seq = mesh.shape["seq"]
    n_head = mesh.shape["head"]
    view = Mesh(mesh.devices.reshape(n_seq // 2, 2, n_head), ("seq_hi", "core", "head"))
    in_specs = (
        P(SEQ, "head"),
        P(None, "head"),
        P(None, "head"),
        P(None, "head"),
        P(SEQ, "head"),
        P(),
    )
    out_specs = (P(SEQ, "head"),) * 4
    return jax.shard_map(
        per_device, mesh=view, in_specs=in_specs, out_specs=out_specs, check_vma=False
    )
```

profile of v0, /device:TPU:27, one launch (start us, length us, event | category | flops | bytes accessed | tf_op | source)
XLA Modules:
  0.0 638.8 jit_solution(9430814455776416603)
XLA Ops:
  13.1 97.3 %all-gather.2.cloned.1.call-done = bf16[512,5376]{0,1:T(8,128)(2,1)} async-done(((bf16[512,1344]{0,1:T(8,128)(2,1)}), bf16[512,5376]{0,1:T(8,128)(2,1)}) %all-gather.2.cloned.1.call-update) | async-done | bytes 5505040 | tf_op jit(solution)/shard_map/all_gather | solution.py:89
  110.5 7.3 %fusion.53 = bf16[1,512,512]{2,1,0:T(8,128)(2,1)S(1)} fusion(bf16[512,5376]{0,1:T(8,128)(2,1)} %all-gather.2.cloned.1.call-done, bf16[5376,512]{1,0:T(8,128)(2,1)} %param.9), kind=kOutput, calls=%fused_computation.77 | convolution fusion | flops 2818834432 | bytes 11534336 | tf_op jit(solution)/shard_map/dot_general | solution.py:96
  117.9 5.7 fusion.52
  123.7 3.4 collective-permute-start.1
  130.3 5.9 convolution_convert_fusion.1
  138.1 9.5 %collective-permute-done.1 = bf16[2,512,512]{2,1,0:T(8,128)(2,1)} collective-permute-done((bf16[2,512,512]{2,1,0:T(8,128)(2,1)S(1)}, bf16[2,512,512]{2,1,0:T(8,128)(2,1)}, u32[]{:S(2)}, u32[]{:S(2)}) %collective-permute-start.1) | collective-permute-done | bytes 1048608 | tf_op jit(solution)/shard_map/ppermute | solution.py:19
  147.5 14.7 %collective-permute-done = bf16[2,512,512]{2,1,0:T(8,128)(2,1)} collective-permute-done((bf16[2,512,512]{2,1,0:T(8,128)(2,1)S(1)}, bf16[2,512,512]{2,1,0:T(8,128)(2,1)}, u32[]{:S(2)}, u32[]{:S(2)}) %collective-permute-start) | collective-permute-done | bytes 1048608 | tf_op jit(solution)/shard_map/ppermute | solution.py:19
  166.7 4.0 reshape_squeeze.7
  170.8 13.6 %fusion.72 = (f32[4,2,512]{2,1,0:T(2,128)S(1)}, f32[4,2,512,1536]{2,3,1,0:T(8,128)}) fusion(pred[512,1536]{0,1:T(8,128)(4,1)S(1)} %copy-done.11, bf16[1536,4,128,1]{0,2,3,1:T(8,128)(2,1)S(1)} %copy.63, bf16[512,4,2,128]{0,3,2,1:T(8,128)(2,1)S(1)} %bitcast.81), kind=kOutput, calls=%fused_computation.110 | convolution fusion | flops 1642071552 | bytes 28590080 | tf_op jit(solution)/shard_map/sub | solution.py:59
  184.3 17.5 %fusion.1 = (f32[4,2,512]{2,1,0:T(2,128)S(1)}, f32[4,1536,512,2]{2,1,3,0:T(8,128)}) fusion(f32[4,2,512,1536]{2,3,1,0:T(8,128)} %get-tuple-element.28, f32[4,2,512]{2,1,0:T(2,128)S(1)} %get-tuple-element.27, bf16[512,4,2,128]{0,3,2,1:T(8,128)(2,1)} %bitcast.83, bf16[1536,4,128,1]{2,1,0,3:T(4,128)(2,1)} %bitcast.82), kind=kOutput, calls=%fused_computation.3 | convolution fusion | flops 1629483008 | bytes 52985856 | tf_op jit(solution)/shard_map/akgd,ckd->kgac/dot_general | solution.py:61
  201.9 17.0 %fusion.3 = bf16[4,2,512,1536]{2,3,1,0:T(8,128)(2,1)S(1)} fusion(f32[4,1536,512,2]{2,1,3,0:T(8,128)} %get-tuple-element.30, f32[4,2,512]{2,1,0:T(2,128)S(1)} %get-tuple-element.29, f32[4,2,512,1536]{2,3,1,0:T(8,128)} %get-tuple-element.28, f32[4,2,512]{2,1,0:T(2,128)S(1)} %get-tuple-element.27), kind=kLoop, calls=%fused_computation.5 | loop fusion | flops 25165824 | bytes 62947328 | tf_op jit(solution)/shard_map/convert_element_type | solution.py:65
  221.7 7.0 %fusion.13 = f32[4,128,1536]{2,1,0:T(8,128)} fusion(bf16[512,4,2,128]{0,3,2,1:T(8,128)(2,1)} %bitcast.80, bf16[4,2,512,1536]{2,3,1,0:T(8,128)(2,1)S(1)} %fusion.3), kind=kOutput, calls=%fused_computation.33 | convolution fusion | flops 1611399168 | bytes 16777216 | tf_op jit(solution)/shard_map/kgac,akgd->ckd/dot_general | solution.py:76
  228.7 11.0 %fusion.5 = f32[4,1536,128,1]{1,2,3,0:T(8,128)S(1)} fusion(bf16[512,4,2,128]{0,3,2,1:T(8,128)(2,1)} %bitcast.84, f32[4,2,512,1536]{2,3,1,0:T(8,128)} %get-tuple-element.28, f32[4,2,512]{2,1,0:T(2,128)S(1)} %get-tuple-element.27), kind=kOutput, calls=%fused_computation.10 | convolution fusion | flops 1623195648 | bytes 29376512 | tf_op jit(solution)/shard_map/kgac,akgd->ckd/dot_general | solution.py:79
  244.7 3.5 fusion.25
  254.7 13.9 %collective-permute-done.3 = bf16[2,512,512]{1,2,0:T(8,128)(2,1)S(1)} collective-permute-done((bf16[2,512,512]{1,2,0:T(8,128)(2,1)S(1)}, bf16[2,512,512]{1,2,0:T(8,128)(2,1)S(1)}, u32[]{:S(2)}, u32[]{:S(2)}) %collective-permute-start.3) | collective-permute-done | bytes 1048608 | tf_op jit(solution)/shard_map/ppermute | solution.py:19
  268.5 3.7 collective-permute-done.2
  282.1 19.3 %convolution_convert_fusion = bf16[2048,5376]{0,1:T(8,128)(2,1)} fusion(bf16[512,5376]{0,1:T(8,128)(2,1)} %all-gather.2.cloned.1.call-done, bf16[512,512]{0,1:T(8,128)(2,1)} %get-tuple-element.26, bf16[512,512]{0,1:T(8,128)(2,1)} %get-tuple-element.25, bf16[512,1024]{0,1:T(8,128)(2,1)S(1)} %bitcast.88), kind=kOutput, calls=%fused_computation.8 | convolution fusion | flops 11291590656 | bytes 29622272 | tf_op jit(solution)/shard_map/dot_general | solution.py:29
  301.4 12.4 %constant_dynamic-slice_fusion.6 = (bf16[2048,672]{0,1:T(8,128)(2,1)}, bf16[2048,672]{0,1:T(8,128)(2,1)S(1)}, bf16[2048,672]{0,1:T(8,128)(2,1)S(1)}, bf16[2048,6...) fusion(bf16[2048,5376]{0,1:T(8,128)(2,1)} %convolution_convert_fusion, ...), kind=kLoop, calls=%fused_computation.89 | loop fusion | bytes 38535196 | tf_op jit(solution)/shard_map/dynamic_slice | solution.py:148
  324.9 85.2 %collective-permute-done.5 = bf16[512,1344]{0,1:T(8,128)(2,1)S(1)} collective-permute-done((bf16[512,1344]{0,1:T(8,128)(2,1)S(1)}, bf16[512,1344]{0,1:T(8,128)(2,1)S(1)}, u32[]{:S(2)}, u32[]{:S(2)}) %collective-permute-start.5) | collective-permute-done | bytes 1376288 | tf_op jit(solution)/shard_map/ppermute | solution.py:138
  413.5 16.9 %collective-permute-done.12 = bf16[2048,672]{0,1:T(8,128)(2,1)} collective-permute-done((bf16[2048,672]{0,1:T(8,128)(2,1)S(1)}, bf16[2048,672]{0,1:T(8,128)(2,1)}, u32[]{:S(2)}, u32[]{:S(2)}) %collective-permute-start.12) | collective-permute-done | bytes 2752544 | tf_op jit(solution)/shard_map/ppermute | solution.py:154
  436.5 3.7 add_convert_fusion
  440.2 149.0 %collective-permute-done.10 = bf16[2048,672]{0,1:T(8,128)(2,1)} collective-permute-done((bf16[2048,672]{0,1:T(8,128)(2,1)}, bf16[2048,672]{0,1:T(8,128)(2,1)}, u32[]{:S(2)}, u32[]{:S(2)}) %collective-permute-start.10) | collective-permute-done | bytes 2752544 | tf_op jit(solution)/shard_map/ppermute | solution.py:154
  589.2 30.1 %collective-permute-done.9 = bf16[2048,672]{0,1:T(8,128)(2,1)} collective-permute-done((bf16[2048,672]{0,1:T(8,128)(2,1)}, bf16[2048,672]{0,1:T(8,128)(2,1)}, u32[]{:S(2)}, u32[]{:S(2)}) %collective-permute-start.9) | collective-permute-done | bytes 2752544 | tf_op jit(solution)/shard_map/ppermute | solution.py:154
  619.3 9.9 %fusion.22 = bf16[672,2048]{1,0:T(8,128)(2,1)S(1)} fusion(bf16[2048,672]{0,1:T(8,128)(2,1)} %collective-permute-done.13, bf16[2048,672]{0,1:T(8,128)(2,1)} %collective-permute-done.12, bf16[2048,672]{0,1:T(8,128)(2,1)} %collective-permute-done.11, bf16[2048,672]{0,1:T(8,128)(2,1)} %collective-permute-done.10, bf16[2048,672]{0,1:T(8,128)(2,1)} %collective-permute-done.9, ...), kind=kLoop, calls=%fused_computation.43 | loop fusion | flops 23396352 | bytes 24772612 | tf_op jit(solution)/shard_map/transpose | solution.py:155
  (92 shorter events, 62.2 us)
Async XLA Ops:
  7.2 103.3 %all-gather.2.cloned.1.call-start = ((), (), s32[]{:S(2)}) async-start(), calls=%async_computation | async-start | bytes 6881280 | tf_op jit(solution)/shard_map/all_gather | solution.py:89
  110.5 19.8 %slice-start = ((s8[11010048]{0:T(1024)(128)(4,1)}), s8[4194304]{0:T(1024)(128)(4,1)S(1)}, s32[]{:S(2)}) async-start(s8[11010048]{0:T(1024)(128)(4,1)} %bitcast.90), calls=%async_computation.1 | async-start | bytes 8388608
  110.5 19.8 %slice-start.1 = ((s8[11010048]{0:T(1024)(128)(4,1)}), s8[4194304]{0:T(1024)(128)(4,1)S(1)}, s32[]{:S(2)}) async-start(s8[11010048]{0:T(1024)(128)(4,1)} %bitcast.90), calls=%async_computation.2 | async-start | bytes 8388608
  117.9 12.5 %slice-start.2 = ((s8[11010048]{0:T(1024)(128)(4,1)}), s8[2621440]{0:T(1024)(128)(4,1)S(1)}, s32[]{:S(2)}) async-start(s8[11010048]{0:T(1024)(128)(4,1)} %bitcast.90), calls=%async_computation.3 | async-start | bytes 5242880
  123.7 23.8 %collective-permute-start.1 = (bf16[2,512,512]{2,1,0:T(8,128)(2,1)S(1)}, bf16[2,512,512]{2,1,0:T(8,128)(2,1)}, u32[]{:S(2)}, u32[]{:S(2)}) collective-permute-start(bf16[2,512,512]{2,1,0:T(8,128)(2,1)S(1)} %pad_maximum_fusion.1), channel_id=1, source_target_pairs={{0,4},{4,8},{8,12},{12,16},{16,20},{20,24},{24,28},{1,5},{5,9},{9,... | collective-permute-start | bytes 3145736 | tf_op jit(solution)/shard_map/ppermute | solution.py:19
  127.2 35.0 %collective-permute-start = (bf16[2,512,512]{2,1,0:T(8,128)(2,1)S(1)}, bf16[2,512,512]{2,1,0:T(8,128)(2,1)}, u32[]{:S(2)}, u32[]{:S(2)}) collective-permute-start(bf16[2,512,512]{2,1,0:T(8,128)(2,1)S(1)} %pad_maximum_fusion.1), channel_id=1, source_target_pairs={{0,8},{4,12},{8,16},{12,20},{16,24},{20,28},{1,9},{5,13},{9,17},{1... | collective-permute-start | bytes 3145736 | tf_op jit(solution)/shard_map/ppermute | solution.py:19
  166.7 17.7 %copy-start.1 = (bf16[1536,4,128,1]{0,2,3,1:T(8,128)(2,1)}, bf16[1536,4,128,1]{0,2,3,1:T(8,128)(2,1)S(1)}, u32[]{:S(2)}) copy-start(bf16[1536,4,128,1]{0,2,3,1:T(8,128)(2,1)S(1)} %copy.63) | copy-start | bytes 4718596
  201.9 17.0 %copy-start.2 = (bf16[1536,4,128,1]{0,2,3,1:T(8,128)(2,1)S(1)}, bf16[1536,4,128,1]{0,2,3,1:T(8,128)(2,1)}, u32[]{:S(2)}) copy-start(bf16[1536,4,128,1]{0,2,3,1:T(8,128)(2,1)} %copy-done.1) | copy-start | bytes 4718596
  228.7 11.0 %copy-start = (f32[4,128,1536]{2,1,0:T(8,128)S(1)}, f32[4,128,1536]{2,1,0:T(8,128)}, u32[]{:S(2)}) copy-start(f32[4,128,1536]{2,1,0:T(8,128)} %fusion.13) | copy-start | bytes 9437188
  240.5 28.0 %collective-permute-start.3 = (bf16[2,512,512]{1,2,0:T(8,128)(2,1)S(1)}, bf16[2,512,512]{1,2,0:T(8,128)(2,1)S(1)}, u32[]{:S(2)}, u32[]{:S(2)}) collective-permute-start(bf16[2,512,512]{1,2,0:T(8,128)(2,1)S(1)} %get-tuple-element.20), channel_id=1, source_target_pairs={{8,0},{12,4},{16,8},{20,12},{24,16},{28,20},{9,1},{13,5},{17,9},{2... | collective-permute-start | bytes 3145736 | tf_op jit(solution)/shard_map/ppermute | solution.py:19
  242.7 29.5 %collective-permute-start.2 = (bf16[2,512,512]{1,2,0:T(8,128)(2,1)S(1)}, bf16[2,512,512]{1,2,0:T(8,128)(2,1)S(1)}, u32[]{:S(2)}, u32[]{:S(2)}) collective-permute-start(bf16[2,512,512]{1,2,0:T(8,128)(2,1)S(1)} %get-tuple-element.19), channel_id=1, source_target_pairs={{4,0},{8,4},{12,8},{16,12},{20,16},{24,20},{28,24},{5,1},{9,5},{13... | collective-permute-start | bytes 3145736 | tf_op jit(solution)/shard_map/ppermute | solution.py:19
  279.3 45.3 %collective-permute-start.6 = (bf16[512,1344]{0,1:T(8,128)(2,1)}, bf16[512,1344]{0,1:T(8,128)(2,1)S(1)}, u32[]{:S(2)}, u32[]{:S(2)}) collective-permute-start(bf16[512,1344]{0,1:T(8,128)(2,1)} %fusion.19), channel_id=1, source_target_pairs={{0,1},{1,2},{2,3},{3,0},{4,5},{5,6},{6,7},{7,4},{8,9},{9,10},{10,1... | collective-permute-start | bytes 4128776 | tf_op jit(solution)/shard_map/ppermute | solution.py:138
  301.4 13.7 %copy-start.5 = (f32[512,1344]{0,1:T(8,128)S(1)}, f32[512,1344]{0,1:T(8,128)}, u32[]{:S(2)}) copy-start(f32[512,1344]{0,1:T(8,128)} %fusion.27) | copy-start | bytes 8257540
  313.9 97.3 %collective-permute-start.13 = (bf16[2048,672]{0,1:T(8,128)(2,1)S(1)}, bf16[2048,672]{0,1:T(8,128)(2,1)}, u32[]{:S(2)}, u32[]{:S(2)}) collective-permute-start(bf16[2048,672]{0,1:T(8,128)(2,1)S(1)} %get-tuple-element.13), channel_id=1, source_target_pairs={{0,4},{4,8},{8,12},{12,16},{16,20},{20,24},{24,28},{28,0},{1,5},{5... | collective-permute-start | bytes 8257544 | tf_op jit(solution)/shard_map/ppermute | solution.py:154
  314.0 116.4 %collective-permute-start.12 = (bf16[2048,672]{0,1:T(8,128)(2,1)S(1)}, bf16[2048,672]{0,1:T(8,128)(2,1)}, u32[]{:S(2)}, u32[]{:S(2)}) collective-permute-start(bf16[2048,672]{0,1:T(8,128)(2,1)S(1)} %get-tuple-element.14), channel_id=1, source_target_pairs={{0,8},{4,12},{8,16},{12,20},{16,24},{20,28},{24,0},{28,4},{1,9},{5... | collective-permute-start | bytes 8257544 | tf_op jit(solution)/shard_map/ppermute | solution.py:154
  319.8 90.4 %collective-permute-start.5 = (bf16[512,1344]{0,1:T(8,128)(2,1)S(1)}, bf16[512,1344]{0,1:T(8,128)(2,1)S(1)}, u32[]{:S(2)}, u32[]{:S(2)}) collective-permute-start(bf16[512,1344]{0,1:T(8,128)(2,1)S(1)} %fusion.18), channel_id=1, source_target_pairs={{0,2},{1,3},{2,0},{3,1},{4,6},{5,7},{6,4},{7,5},{8,10},{9,11},{10,... | collective-permute-start | bytes 4128776 | tf_op jit(solution)/shard_map/ppermute | solution.py:138
  324.3 85.8 %collective-permute-start.4 = (bf16[512,1344]{0,1:T(8,128)(2,1)S(1)}, bf16[512,1344]{0,1:T(8,128)(2,1)S(1)}, u32[]{:S(2)}, u32[]{:S(2)}) collective-permute-start(bf16[512,1344]{0,1:T(8,128)(2,1)S(1)} %fusion.17), channel_id=1, source_target_pairs={{0,3},{1,0},{2,1},{3,2},{4,7},{5,4},{6,5},{7,6},{8,11},{9,8},{10,9... | collective-permute-start | bytes 4128776 | tf_op jit(solution)/shard_map/ppermute | solution.py:138
  324.6 115.6 %collective-permute-start.11 = (bf16[2048,672]{0,1:T(8,128)(2,1)}, bf16[2048,672]{0,1:T(8,128)(2,1)}, u32[]{:S(2)}, u32[]{:S(2)}) collective-permute-start(bf16[2048,672]{0,1:T(8,128)(2,1)} %get-tuple-element.15), channel_id=1, source_target_pairs={{0,12},{4,16},{8,20},{12,24},{16,28},{20,0},{24,4},{28,8},{1,13},{... | collective-permute-start | bytes 8257544 | tf_op jit(solution)/shard_map/ppermute | solution.py:154
  410.1 20.2 %copy-start.6 = (bf16[512,1344]{0,1:T(8,128)(2,1)}, bf16[512,1344]{0,1:T(8,128)(2,1)S(1)}, u32[]{:S(2)}) copy-start(bf16[512,1344]{0,1:T(8,128)(2,1)S(1)} %collective-permute-done.5) | copy-start | bytes 4128772
  410.1 179.0 %collective-permute-start.10 = (bf16[2048,672]{0,1:T(8,128)(2,1)}, bf16[2048,672]{0,1:T(8,128)(2,1)}, u32[]{:S(2)}, u32[]{:S(2)}) collective-permute-start(bf16[2048,672]{0,1:T(8,128)(2,1)} %get-tuple-element.16), channel_id=1, source_target_pairs={{0,16},{4,20},{8,24},{12,28},{16,0},{20,4},{24,8},{28,12},{1,17},{... | collective-permute-start | bytes 8257544 | tf_op jit(solution)/shard_map/ppermute | solution.py:154
  410.2 20.2 %copy-start.8 = (bf16[512,1344]{0,1:T(8,128)(2,1)}, bf16[512,1344]{0,1:T(8,128)(2,1)S(1)}, u32[]{:S(2)}) copy-start(bf16[512,1344]{0,1:T(8,128)(2,1)S(1)} %collective-permute-done.4) | copy-start | bytes 4128772
  410.2 209.2 %collective-permute-start.9 = (bf16[2048,672]{0,1:T(8,128)(2,1)}, bf16[2048,672]{0,1:T(8,128)(2,1)}, u32[]{:S(2)}, u32[]{:S(2)}) collective-permute-start(bf16[2048,672]{0,1:T(8,128)(2,1)} %get-tuple-element.17), channel_id=1, source_target_pairs={{0,20},{4,24},{8,28},{12,0},{16,4},{20,8},{24,12},{28,16},{1,21},{... | collective-permute-start | bytes 8257544 | tf_op jit(solution)/shard_map/ppermute | solution.py:154
  411.1 208.2 %collective-permute-start.8 = (bf16[2048,672]{0,1:T(8,128)(2,1)}, bf16[2048,672]{0,1:T(8,128)(2,1)}, u32[]{:S(2)}, u32[]{:S(2)}) collective-permute-start(bf16[2048,672]{0,1:T(8,128)(2,1)} %get-tuple-element.18), channel_id=1, source_target_pairs={{0,24},{4,28},{8,0},{12,4},{16,8},{20,12},{24,16},{28,20},{1,25},{... | collective-permute-start | bytes 8257544 | tf_op jit(solution)/shard_map/ppermute | solution.py:154
  430.4 188.9 %collective-permute-start.7 = (bf16[2048,672]{0,1:T(8,128)(2,1)}, bf16[2048,672]{0,1:T(8,128)(2,1)}, u32[]{:S(2)}, u32[]{:S(2)}) collective-permute-start(bf16[2048,672]{0,1:T(8,128)(2,1)} %get-tuple-element.12), channel_id=1, source_target_pairs={{0,28},{4,0},{8,4},{12,8},{16,12},{20,16},{24,20},{28,24},{1,29},{... | collective-permute-start | bytes 8257544 | tf_op jit(solution)/shard_map/ppermute | solution.py:154
  (11 other events, 51.0 us)
Sparse Core Ops, SparseCore 0:
  9.6 100.8 all-gather.1
where the time goes:
time: 646 us; the launch traced here: 639 us
  waiting for transfers between devices  421 us (65%)
  matrix products  124 us (19%)
  other arithmetic  32.4 us (5%)
  local copies, waits for them, and re-layouts  27.2 us (4%)
  starting transfers between devices  19 us (3%)
  between operations  14.9 us (2%)
    ppermute x7, waiting for transfers between devices, per_device(): weight_sum = weight_sum + lax.ppermute(sent, SEQ, pairs).astype(jnp.float32)  196 us
    all_gather x1, waiting for transfers between devices, per_device(): gathered = lax.all_gather(tokens, 'head', axis=1, tiled=True)  97.3 us
    ppermute x3, waiting for transfers between devices, per_device(): got = lax.ppermute(sent, 'head', pairs).astype(jnp.float32)  85.2 us
    ppermute x4, waiting for transfers between devices, passed_along(): return lax.ppermute(x, axis, pairs)  41.7 us
    dot_general x12, matrix products, contract_last(): lax.dot_general(left, right, (((1,), (1,)), ((), ())), preferred_element_...  34 us
    dot_general x1, matrix products, contract_first(): lax.dot_general(left, right, (((0,), (0,)), ((), ())), preferred_element_...  19.3 us
    dot_general x1, matrix products, attend(): jnp.einsum('akgd,ckd->kgac', grad_four, value_three, preferred_element_ty...  17.5 us
    convert_element_type x1, other arithmetic, attend(): dscores = (probs * (dprobs - center)).astype(jnp.bfloat16)  17 us
  transfers between devices with their start and end apart: 15, of which 9 were waited for; matrix products, arithmetic and copies ran while one was open for 11% of the time, Pallas kernels for 0%

commit v1 on v0

--- a/solution.py
+++ b/solution.py
@@ -86,7 +86,12 @@
     tok_rows = tokens.shape[0]
     hop_count = HOPS
     margin = hop_count * tok_rows
-    gathered = lax.all_gather(tokens, "head", axis=1, tiled=True)
+    ring = [tokens]
+    for hop in range(3):
+        ring.append(lax.ppermute(ring[-1], "head", [(dev, (dev + 1) % 4) for dev in range(4)]))
+    gathered = jnp.roll(
+        jnp.concatenate(ring[::-1], axis=1), (lax.axis_index("head") + 1) * ring[0].shape[1], axis=1
+    )
     queries = jnp.dot(gathered, query_weight, preferred_element_type=jnp.float32).astype(
         jnp.bfloat16
     )

time: 646 us -> 623 us (0.964)
  waiting for transfers between devices: 421 us -> 401 us
  between operations: 14.9 us -> 1.69 us
  starting transfers between devices: 19 us -> 29.7 us
  local copies, waits for them, and re-layouts: 27.2 us -> 34.8 us
  matrix products: 124 us -> 117 us
    all_gather x1 -> x0, waiting for transfers between devices: 97.3 us -> none  [per_device(): gathered = lax.all_gather(tokens, 'head', axis=1, tiled=True)]
    ppermute x0 -> x3, waiting for transfers between devices: none -> 80.1 us  [per_device(): lax.ppermute(ring[-1], 'head', [(dev, (dev + 1) % 4) for dev in range(4)])]
  transfers between devices with their start and end apart: 15 -> 17, of which waited for: 9 -> 11; matrix products, arithmetic and copies ran while one was open for 11% -> 12% of each run, Pallas kernels for 0% -> 0%
where the time goes in v1:
time: 623 us; the launch traced here: 616 us
  waiting for transfers between devices  401 us (64%)
  matrix products  117 us (19%)
  local copies, waits for them, and re-layouts  34.8 us (6%)
  other arithmetic  33.1 us (5%)
  starting transfers between devices  29.7 us (5%)
    ppermute x7, waiting for transfers between devices, per_device(): weight_sum = weight_sum + lax.ppermute(sent, SEQ, pairs).astype(jnp.float32)  196 us
    ppermute x3, waiting for transfers between devices, per_device(): got = lax.ppermute(sent, 'head', pairs).astype(jnp.float32)  84.5 us
    ppermute x3, waiting for transfers between devices, per_device(): lax.ppermute(ring[-1], 'head', [(dev, (dev + 1) % 4) for dev in range(4)])  80.1 us
    ppermute x4, waiting for transfers between devices, passed_along(): return lax.ppermute(x, axis, pairs)  40 us
    dot_general x12, matrix products, contract_last(): lax.dot_general(left, right, (((1,), (1,)), ((), ())), preferred_element_...  34 us
    dot_general x1, matrix products, contract_first(): lax.dot_general(left, right, (((0,), (0,)), ((), ())), preferred_element_...  18.2 us
    dot_general x1, matrix products, attend(): jnp.einsum('akgd,ckd->kgac', grad_four, value_three, preferred_element_ty...  17.8 us
    convert_element_type x1, other arithmetic, attend(): dscores = (probs * (dprobs - center)).astype(jnp.bfloat16)  17 us
  transfers between devices with their start and end apart: 17, of which 11 were waited for; matrix products, arithmetic and copies ran while one was open for 12% of the time, Pallas kernels for 0%

profile of v1, /device:TPU:27, one launch (start us, length us, event | category | flops | bytes accessed | tf_op | source)
XLA Modules:
  0.0 616.4 jit_solution(6274446812092865056)
XLA Ops:
  0.7 31.2 %collective-permute-done = bf16[512,1344]{0,1:T(8,128)(2,1)S(1)} collective-permute-done((bf16[512,1344]{0,1:T(8,128)(2,1)}, bf16[512,1344]{0,1:T(8,128)(2,1)S(1)}, u32[]{:S(2)}, u32[]{:S(2)}) %collective-permute-start) | collective-permute-done | bytes 1376288 | tf_op jit(solution)/shard_map/ppermute | solution.py:91
  33.8 28.2 %collective-permute-done.1 = bf16[512,1344]{0,1:T(8,128)(2,1)S(1)} collective-permute-done((bf16[512,1344]{0,1:T(8,128)(2,1)S(1)}, bf16[512,1344]{0,1:T(8,128)(2,1)S(1)}, u32[]{:S(2)}, u32[]{:S(2)}) %collective-permute-start.1) | collective-permute-done | bytes 1376288 | tf_op jit(solution)/shard_map/ppermute | solution.py:91
  62.1 3.8 collective-permute-start.2
  72.3 20.6 %collective-permute-done.2 = bf16[512,1344]{0,1:T(8,128)(2,1)} collective-permute-done((bf16[512,1344]{0,1:T(8,128)(2,1)S(1)}, bf16[512,1344]{0,1:T(8,128)(2,1)}, u32[]{:S(2)}, u32[]{:S(2)}) %collective-permute-start.2) | collective-permute-done | bytes 1376288 | tf_op jit(solution)/shard_map/ppermute | solution.py:91
  105.2 6.6 %collective-permute-start.4 = (bf16[2,512,512]{2,1,0:T(8,128)(2,1)S(1)}, bf16[2,512,512]{2,1,0:T(8,128)(2,1)}, u32[]{:S(2)}, u32[]{:S(2)}) collective-permute-start(bf16[2,512,512]{2,1,0:T(8,128)(2,1)S(1)} %pad_maximum_fusion.1), channel_id=1, source_target_pairs={{0,4},{4,8},{8,12},{12,16},{16,20},{20,24},{24,28},{1,5},{5,9},{9,... | collective-permute-start | bytes 3145736 | tf_op jit(solution)/shard_map/ppermute | solution.py:19
  115.5 5.9 fusion.49
  124.3 7.8 %collective-permute-done.4 = bf16[2,512,512]{2,1,0:T(8,128)(2,1)} collective-permute-done((bf16[2,512,512]{2,1,0:T(8,128)(2,1)S(1)}, bf16[2,512,512]{2,1,0:T(8,128)(2,1)}, u32[]{:S(2)}, u32[]{:S(2)}) %collective-permute-start.4) | collective-permute-done | bytes 1048608 | tf_op jit(solution)/shard_map/ppermute | solution.py:19
  132.1 14.6 %collective-permute-done.3 = bf16[2,512,512]{2,1,0:T(8,128)(2,1)} collective-permute-done((bf16[2,512,512]{2,1,0:T(8,128)(2,1)S(1)}, bf16[2,512,512]{2,1,0:T(8,128)(2,1)}, u32[]{:S(2)}, u32[]{:S(2)}) %collective-permute-start.3) | collective-permute-done | bytes 1048608 | tf_op jit(solution)/shard_map/ppermute | solution.py:19
  151.3 4.0 reshape_squeeze.7
  155.3 13.6 %fusion.96 = (f32[4,2,512]{2,1,0:T(2,128)S(1)}, f32[4,2,512,1536]{2,3,1,0:T(8,128)}) fusion(pred[512,1536]{0,1:T(8,128)(4,1)S(1)} %copy-done.12, bf16[1536,4,128,1]{0,2,3,1:T(8,128)(2,1)S(1)} %copy.63, bf16[512,4,2,128]{0,3,2,1:T(8,128)(2,1)S(1)} %bitcast.81), kind=kOutput, calls=%fused_computation.129 | convolution fusion | flops 1642071552 | bytes 28590080 | tf_op jit(solution)/shard_map/sub | solution.py:59
  168.9 17.8 %fusion.1 = (f32[4,2,512]{2,1,0:T(2,128)S(1)}, f32[4,1536,512,2]{2,1,3,0:T(8,128)}) fusion(f32[4,2,512,1536]{2,3,1,0:T(8,128)} %get-tuple-element.28, f32[4,2,512]{2,1,0:T(2,128)S(1)} %get-tuple-element.27, bf16[512,4,2,128]{0,3,2,1:T(8,128)(2,1)} %bitcast.83, bf16[1536,4,128,1]{2,1,0,3:T(4,128)(2,1)} %bitcast.82), kind=kOutput, calls=%fused_computation.3 | convolution fusion | flops 1629483008 | bytes 52985856 | tf_op jit(solution)/shard_map/akgd,ckd->kgac/dot_general | solution.py:61
  186.7 17.0 %fusion.3 = bf16[4,2,512,1536]{2,3,1,0:T(8,128)(2,1)S(1)} fusion(f32[4,1536,512,2]{2,1,3,0:T(8,128)} %get-tuple-element.30, f32[4,2,512]{2,1,0:T(2,128)S(1)} %get-tuple-element.29, f32[4,2,512,1536]{2,3,1,0:T(8,128)} %get-tuple-element.28, f32[4,2,512]{2,1,0:T(2,128)S(1)} %get-tuple-element.27), kind=kLoop, calls=%fused_computation.5 | loop fusion | flops 25165824 | bytes 62947328 | tf_op jit(solution)/shard_map/convert_element_type | solution.py:65
  206.6 7.0 %fusion.20 = f32[4,128,1536]{2,1,0:T(8,128)} fusion(bf16[512,4,2,128]{0,3,2,1:T(8,128)(2,1)} %bitcast.80, bf16[4,2,512,1536]{2,3,1,0:T(8,128)(2,1)S(1)} %fusion.3), kind=kOutput, calls=%fused_computation.40 | convolution fusion | flops 1611399168 | bytes 16777216 | tf_op jit(solution)/shard_map/kgac,akgd->ckd/dot_general | solution.py:76
  213.5 11.0 %fusion.5 = f32[4,1536,128,1]{1,2,3,0:T(8,128)S(1)} fusion(bf16[512,4,2,128]{0,3,2,1:T(8,128)(2,1)} %bitcast.84, f32[4,2,512,1536]{2,3,1,0:T(8,128)} %get-tuple-element.28, f32[4,2,512]{2,1,0:T(2,128)S(1)} %get-tuple-element.27), kind=kOutput, calls=%fused_computation.10 | convolution fusion | flops 1623195648 | bytes 29376512 | tf_op jit(solution)/shard_map/kgac,akgd->ckd/dot_general | solution.py:79
  239.5 13.9 %collective-permute-done.6 = bf16[2,512,512]{1,2,0:T(8,128)(2,1)S(1)} collective-permute-done((bf16[2,512,512]{1,2,0:T(8,128)(2,1)S(1)}, bf16[2,512,512]{1,2,0:T(8,128)(2,1)S(1)}, u32[]{:S(2)}, u32[]{:S(2)}) %collective-permute-start.6) | collective-permute-done | bytes 1048608 | tf_op jit(solution)/shard_map/ppermute | solution.py:19
  264.1 4.1 collective-permute-start.9
  268.2 18.2 %convolution_convert_fusion = bf16[2048,5376]{0,1:T(8,128)(2,1)} fusion(bf16[512,10752]{0,1:T(8,128)(2,1)} %copy-done.13, s32[]{:T(128)S(6)} %select_n.113, bf16[512,512]{0,1:T(8,128)(2,1)} %get-tuple-element.26, bf16[512,512]{0,1:T(8,128)(2,1)} %get-tuple-element.25, bf16[512,1024]{0,1:T(8,128)(2,1)S(1)} %bitcast.88), kind=kOutput, calls=%fused_computation.8 | convolution fusion | flops 11291590656 | bytes 29622276 | tf_op jit(solution)/shard_map/dot_general | solution.py:29
  286.4 12.4 %constant_dynamic-slice_fusion.6 = (bf16[2048,672]{0,1:T(8,128)(2,1)}, bf16[2048,672]{0,1:T(8,128)(2,1)S(1)}, bf16[2048,672]{0,1:T(8,128)(2,1)S(1)}, bf16[2048,6...) fusion(bf16[2048,5376]{0,1:T(8,128)(2,1)} %convolution_convert_fusion, ...), kind=kLoop, calls=%fused_computation.107 | loop fusion | bytes 38535196 | tf_op jit(solution)/shard_map/dynamic_slice | solution.py:153
  309.9 84.5 %collective-permute-done.8 = bf16[512,1344]{0,1:T(8,128)(2,1)S(1)} collective-permute-done((bf16[512,1344]{0,1:T(8,128)(2,1)S(1)}, bf16[512,1344]{0,1:T(8,128)(2,1)S(1)}, u32[]{:S(2)}, u32[]{:S(2)}) %collective-permute-start.8) | collective-permute-done | bytes 1376288 | tf_op jit(solution)/shard_map/ppermute | solution.py:143
  397.8 17.6 %collective-permute-done.15 = bf16[2048,672]{0,1:T(8,128)(2,1)} collective-permute-done((bf16[2048,672]{0,1:T(8,128)(2,1)S(1)}, bf16[2048,672]{0,1:T(8,128)(2,1)}, u32[]{:S(2)}, u32[]{:S(2)}) %collective-permute-start.15) | collective-permute-done | bytes 2752544 | tf_op jit(solution)/shard_map/ppermute | solution.py:159
  421.5 3.7 add_convert_fusion
  425.2 148.3 %collective-permute-done.13 = bf16[2048,672]{0,1:T(8,128)(2,1)} collective-permute-done((bf16[2048,672]{0,1:T(8,128)(2,1)}, bf16[2048,672]{0,1:T(8,128)(2,1)}, u32[]{:S(2)}, u32[]{:S(2)}) %collective-permute-start.13) | collective-permute-done | bytes 2752544 | tf_op jit(solution)/shard_map/ppermute | solution.py:159
  573.5 30.1 %collective-permute-done.12 = bf16[2048,672]{0,1:T(8,128)(2,1)} collective-permute-done((bf16[2048,672]{0,1:T(8,128)(2,1)}, bf16[2048,672]{0,1:T(8,128)(2,1)}, u32[]{:S(2)}, u32[]{:S(2)}) %collective-permute-start.12) | collective-permute-done | bytes 2752544 | tf_op jit(solution)/shard_map/ppermute | solution.py:159
  603.6 9.9 %fusion.29 = bf16[672,2048]{1,0:T(8,128)(2,1)S(1)} fusion(bf16[2048,672]{0,1:T(8,128)(2,1)} %collective-permute-done.16, bf16[2048,672]{0,1:T(8,128)(2,1)} %collective-permute-done.15, bf16[2048,672]{0,1:T(8,128)(2,1)} %collective-permute-done.14, bf16[2048,672]{0,1:T(8,128)(2,1)} %collective-permute-done.13, bf16[2048,672]{0,1:T(8,128)(2,1)} %collective-permute-done.12, ...), kind=kLoop, calls=%fused_computation.50 | loop fusion | flops 23396352 | bytes 24772612 | tf_op jit(solution)/shard_map/transpose | solution.py:160
  (113 shorter events, 82.8 us)
Async XLA Ops:
  0.6 31.3 %collective-permute-start = (bf16[512,1344]{0,1:T(8,128)(2,1)}, bf16[512,1344]{0,1:T(8,128)(2,1)S(1)}, u32[]{:S(2)}, u32[]{:S(2)}) collective-permute-start(bf16[512,1344]{0,1:T(8,128)(2,1)} %param.6), channel_id=1, source_target_pairs={{0,1},{1,2},{2,3},{3,0},{4,5},{5,6},{6,7},{7,4},{8,9},{9,10},{10,1... | collective-permute-start | bytes 4128776 | tf_op jit(solution)/shard_map/ppermute | solution.py:91
  31.9 30.1 %collective-permute-start.1 = (bf16[512,1344]{0,1:T(8,128)(2,1)S(1)}, bf16[512,1344]{0,1:T(8,128)(2,1)S(1)}, u32[]{:S(2)}, u32[]{:S(2)}) collective-permute-start(bf16[512,1344]{0,1:T(8,128)(2,1)S(1)} %collective-permute-done), channel_id=1, source_target_pairs={{0,1},{1,2},{2,3},{3,0},{4,5},{5,6},{6,7},{7,4},{8,9},{9,10},{10,1... | collective-permute-start | bytes 4128776 | tf_op jit(solution)/shard_map/ppermute | solution.py:91
  62.1 30.8 %collective-permute-start.2 = (bf16[512,1344]{0,1:T(8,128)(2,1)S(1)}, bf16[512,1344]{0,1:T(8,128)(2,1)}, u32[]{:S(2)}, u32[]{:S(2)}) collective-permute-start(bf16[512,1344]{0,1:T(8,128)(2,1)S(1)} %collective-permute-done.1), channel_id=1, source_target_pairs={{0,1},{1,2},{2,3},{3,0},{4,5},{5,6},{6,7},{7,4},{8,9},{9,10},{10,1... | collective-permute-start | bytes 4128776 | tf_op jit(solution)/shard_map/ppermute | solution.py:91
  98.9 16.5 %copy-start.13 = (bf16[512,10752]{0,1:T(8,128)(2,1)}, bf16[512,10752]{0,1:T(8,128)(2,1)S(1)}, u32[]{:S(2)}) copy-start(bf16[512,10752]{0,1:T(8,128)(2,1)S(1)} %constant_dynamic-update-slice_fusion) | copy-start | bytes 33030148
  98.9 16.5 %slice-start.4 = ((s8[11010048]{0:T(1024)(128)(4,1)}), s8[4194304]{0:T(1024)(128)(4,1)S(1)}, s32[]{:S(2)}) async-start(s8[11010048]{0:T(1024)(128)(4,1)} %bitcast.90), calls=%async_computation.4 | async-start | bytes 8388608
  98.9 16.5 %slice-start.5 = ((s8[11010048]{0:T(1024)(128)(4,1)}), s8[4194304]{0:T(1024)(128)(4,1)S(1)}, s32[]{:S(2)}) async-start(s8[11010048]{0:T(1024)(128)(4,1)} %bitcast.90), calls=%async_computation.5 | async-start | bytes 8388608
  105.2 27.0 %collective-permute-start.4 = (bf16[2,512,512]{2,1,0:T(8,128)(2,1)S(1)}, bf16[2,512,512]{2,1,0:T(8,128)(2,1)}, u32[]{:S(2)}, u32[]{:S(2)}) collective-permute-start(bf16[2,512,512]{2,1,0:T(8,128)(2,1)S(1)} %pad_maximum_fusion.1), channel_id=1, source_target_pairs={{0,4},{4,8},{8,12},{12,16},{16,20},{20,24},{24,28},{1,5},{5,9},{9,... | collective-permute-start | bytes 3145736 | tf_op jit(solution)/shard_map/ppermute | solution.py:19
  111.8 35.0 %collective-permute-start.3 = (bf16[2,512,512]{2,1,0:T(8,128)(2,1)S(1)}, bf16[2,512,512]{2,1,0:T(8,128)(2,1)}, u32[]{:S(2)}, u32[]{:S(2)}) collective-permute-start(bf16[2,512,512]{2,1,0:T(8,128)(2,1)S(1)} %pad_maximum_fusion.1), channel_id=1, source_target_pairs={{0,8},{4,12},{8,16},{12,20},{16,24},{20,28},{1,9},{5,13},{9,17},{1... | collective-permute-start | bytes 3145736 | tf_op jit(solution)/shard_map/ppermute | solution.py:19
  151.3 17.6 %copy-start.1 = (bf16[1536,4,128,1]{0,2,3,1:T(8,128)(2,1)}, bf16[1536,4,128,1]{0,2,3,1:T(8,128)(2,1)S(1)}, u32[]{:S(2)}) copy-start(bf16[1536,4,128,1]{0,2,3,1:T(8,128)(2,1)S(1)} %copy.63) | copy-start | bytes 4718596
  186.7 17.0 %copy-start.2 = (bf16[1536,4,128,1]{0,2,3,1:T(8,128)(2,1)S(1)}, bf16[1536,4,128,1]{0,2,3,1:T(8,128)(2,1)}, u32[]{:S(2)}) copy-start(bf16[1536,4,128,1]{0,2,3,1:T(8,128)(2,1)} %copy-done.1) | copy-start | bytes 4718596
  225.4 28.0 %collective-permute-start.6 = (bf16[2,512,512]{1,2,0:T(8,128)(2,1)S(1)}, bf16[2,512,512]{1,2,0:T(8,128)(2,1)S(1)}, u32[]{:S(2)}, u32[]{:S(2)}) collective-permute-start(bf16[2,512,512]{1,2,0:T(8,128)(2,1)S(1)} %get-tuple-element.20), channel_id=1, source_target_pairs={{8,0},{12,4},{16,8},{20,12},{24,16},{28,20},{9,1},{13,5},{17,9},{2... | collective-permute-start | bytes 3145736 | tf_op jit(solution)/shard_map/ppermute | solution.py:19
  227.6 29.5 %collective-permute-start.5 = (bf16[2,512,512]{1,2,0:T(8,128)(2,1)S(1)}, bf16[2,512,512]{1,2,0:T(8,128)(2,1)S(1)}, u32[]{:S(2)}, u32[]{:S(2)}) collective-permute-start(bf16[2,512,512]{1,2,0:T(8,128)(2,1)S(1)} %get-tuple-element.19), channel_id=1, source_target_pairs={{4,0},{8,4},{12,8},{16,12},{20,16},{24,20},{28,24},{5,1},{9,5},{13... | collective-permute-start | bytes 3145736 | tf_op jit(solution)/shard_map/ppermute | solution.py:19
  264.1 45.5 %collective-permute-start.9 = (bf16[512,1344]{0,1:T(8,128)(2,1)}, bf16[512,1344]{0,1:T(8,128)(2,1)S(1)}, u32[]{:S(2)}, u32[]{:S(2)}) collective-permute-start(bf16[512,1344]{0,1:T(8,128)(2,1)} %fusion.26), channel_id=1, source_target_pairs={{0,1},{1,2},{2,3},{3,0},{4,5},{5,6},{6,7},{7,4},{8,9},{9,10},{10,1... | collective-permute-start | bytes 4128776 | tf_op jit(solution)/shard_map/ppermute | solution.py:143
  298.9 96.6 %collective-permute-start.16 = (bf16[2048,672]{0,1:T(8,128)(2,1)S(1)}, bf16[2048,672]{0,1:T(8,128)(2,1)}, u32[]{:S(2)}, u32[]{:S(2)}) collective-permute-start(bf16[2048,672]{0,1:T(8,128)(2,1)S(1)} %get-tuple-element.13), channel_id=1, source_target_pairs={{0,4},{4,8},{8,12},{12,16},{16,20},{20,24},{24,28},{28,0},{1,5},{5... | collective-permute-start | bytes 8257544 | tf_op jit(solution)/shard_map/ppermute | solution.py:159
  299.0 116.4 %collective-permute-start.15 = (bf16[2048,672]{0,1:T(8,128)(2,1)S(1)}, bf16[2048,672]{0,1:T(8,128)(2,1)}, u32[]{:S(2)}, u32[]{:S(2)}) collective-permute-start(bf16[2048,672]{0,1:T(8,128)(2,1)S(1)} %get-tuple-element.14), channel_id=1, source_target_pairs={{0,8},{4,12},{8,16},{12,20},{16,24},{20,28},{24,0},{28,4},{1,9},{5... | collective-permute-start | bytes 8257544 | tf_op jit(solution)/shard_map/ppermute | solution.py:159
  304.8 89.6 %collective-permute-start.8 = (bf16[512,1344]{0,1:T(8,128)(2,1)S(1)}, bf16[512,1344]{0,1:T(8,128)(2,1)S(1)}, u32[]{:S(2)}, u32[]{:S(2)}) collective-permute-start(bf16[512,1344]{0,1:T(8,128)(2,1)S(1)} %fusion.25), channel_id=1, source_target_pairs={{0,2},{1,3},{2,0},{3,1},{4,6},{5,7},{6,4},{7,5},{8,10},{9,11},{10,... | collective-permute-start | bytes 4128776 | tf_op jit(solution)/shard_map/ppermute | solution.py:143
  309.4 85.1 %collective-permute-start.7 = (bf16[512,1344]{0,1:T(8,128)(2,1)S(1)}, bf16[512,1344]{0,1:T(8,128)(2,1)S(1)}, u32[]{:S(2)}, u32[]{:S(2)}) collective-permute-start(bf16[512,1344]{0,1:T(8,128)(2,1)S(1)} %fusion.24), channel_id=1, source_target_pairs={{0,3},{1,0},{2,1},{3,2},{4,7},{5,4},{6,5},{7,6},{8,11},{9,8},{10,9... | collective-permute-start | bytes 4128776 | tf_op jit(solution)/shard_map/ppermute | solution.py:143
  309.6 115.6 %collective-permute-start.14 = (bf16[2048,672]{0,1:T(8,128)(2,1)}, bf16[2048,672]{0,1:T(8,128)(2,1)}, u32[]{:S(2)}, u32[]{:S(2)}) collective-permute-start(bf16[2048,672]{0,1:T(8,128)(2,1)} %get-tuple-element.15), channel_id=1, source_target_pairs={{0,12},{4,16},{8,20},{12,24},{16,28},{20,0},{24,4},{28,8},{1,13},{... | collective-permute-start | bytes 8257544 | tf_op jit(solution)/shard_map/ppermute | solution.py:159
  394.5 20.9 %copy-start.7 = (bf16[512,1344]{0,1:T(8,128)(2,1)}, bf16[512,1344]{0,1:T(8,128)(2,1)S(1)}, u32[]{:S(2)}) copy-start(bf16[512,1344]{0,1:T(8,128)(2,1)S(1)} %collective-permute-done.8) | copy-start | bytes 4128772
  394.5 179.0 %collective-permute-start.13 = (bf16[2048,672]{0,1:T(8,128)(2,1)}, bf16[2048,672]{0,1:T(8,128)(2,1)}, u32[]{:S(2)}, u32[]{:S(2)}) collective-permute-start(bf16[2048,672]{0,1:T(8,128)(2,1)} %get-tuple-element.16), channel_id=1, source_target_pairs={{0,16},{4,20},{8,24},{12,28},{16,0},{20,4},{24,8},{28,12},{1,17},{... | collective-permute-start | bytes 8257544 | tf_op jit(solution)/shard_map/ppermute | solution.py:159
  394.5 20.9 %copy-start.9 = (bf16[512,1344]{0,1:T(8,128)(2,1)}, bf16[512,1344]{0,1:T(8,128)(2,1)S(1)}, u32[]{:S(2)}) copy-start(bf16[512,1344]{0,1:T(8,128)(2,1)S(1)} %collective-permute-done.7) | copy-start | bytes 4128772
  394.5 209.2 %collective-permute-start.12 = (bf16[2048,672]{0,1:T(8,128)(2,1)}, bf16[2048,672]{0,1:T(8,128)(2,1)}, u32[]{:S(2)}, u32[]{:S(2)}) collective-permute-start(bf16[2048,672]{0,1:T(8,128)(2,1)} %get-tuple-element.17), channel_id=1, source_target_pairs={{0,20},{4,24},{8,28},{12,0},{16,4},{20,8},{24,12},{28,16},{1,21},{... | collective-permute-start | bytes 8257544 | tf_op jit(solution)/shard_map/ppermute | solution.py:159
  395.4 208.2 %collective-permute-start.11 = (bf16[2048,672]{0,1:T(8,128)(2,1)}, bf16[2048,672]{0,1:T(8,128)(2,1)}, u32[]{:S(2)}, u32[]{:S(2)}) collective-permute-start(bf16[2048,672]{0,1:T(8,128)(2,1)} %get-tuple-element.18), channel_id=1, source_target_pairs={{0,24},{4,28},{8,0},{12,4},{16,8},{20,12},{24,16},{28,20},{1,25},{... | collective-permute-start | bytes 8257544 | tf_op jit(solution)/shard_map/ppermute | solution.py:159
  415.4 188.3 %collective-permute-start.10 = (bf16[2048,672]{0,1:T(8,128)(2,1)}, bf16[2048,672]{0,1:T(8,128)(2,1)}, u32[]{:S(2)}, u32[]{:S(2)}) collective-permute-start(bf16[2048,672]{0,1:T(8,128)(2,1)} %get-tuple-element.12), channel_id=1, source_target_pairs={{0,28},{4,0},{8,4},{12,8},{16,12},{20,16},{24,20},{28,24},{1,29},{... | collective-permute-start | bytes 8257544 | tf_op jit(solution)/shard_map/ppermute | solution.py:159
  (17 other events, 91.6 us)
